TPU v7x, 256 devices: a whole 4x4x8 slice. The times are simulated.
256 devices in a mesh: rep: 32 (over x, y, core), tp: 8 (over z).
Axes of the slice: x: 4, y: 4, z: 8, core: 2. Of those that a mesh axis runs over, the one named last changes fastest.
Arguments:
- prompt_rows: bfloat16 [20480, 2048], P(('rep', 'tp')), may hold values from -6 to 6
- prompt_pieces: int32 [32, 640], P('rep'), may hold values from 0 to 9, never falling along the last dimension, each value on 1 to 320 neighbouring positions
- decode_rows: bfloat16 [1280, 2048], P('rep'), may hold values from -6 to 6
- request_ages: int32 [1280], P('rep'), may hold values from 2 to 127
- migrate_to: int32 [512, 1], P('rep'), may hold values from 0 to 31, as said below
- past_cache: bfloat16 [1280, 2, 128, 2048], P('rep', None, None, 'tp'), may hold values from -8 to 8
- norm_gain: float32 [2048], replicated, may hold values from 0.5 to 1.5
- norm_bias: float32 [2048], replicated, may hold values from -2 to 2
- qkv_weight: bfloat16 [3, 2048, 2048], P(None, None, 'tp'), may hold values from -0.125 to 0.125
- qkv_bias: float32 [3, 2048], P(None, 'tp'), may hold values from -4 to 4
- out_weight: bfloat16 [2048, 2048], P('tp'), may hold values from -0.125 to 0.125
- out_bias: float32 [2048], replicated, may hold values from -3 to 3
Outputs:
- prompt_out: bfloat16 [20480, 2048], P(('rep', 'tp'))
- prompt_cache: bfloat16 [2, 20480, 2048], P(None, 'rep', 'tp')
- kept_out: bfloat16 [768, 2048], P('rep')
- kept_cache: bfloat16 [768, 2, 128, 2048], P('rep', None, None, 'tp')
- moved_out: bfloat16 [1024, 2048], P('rep')
- moved_cache: bfloat16 [1024, 2, 128, 2048], P('rep', None, None, 'tp')
Inputs may be any that keep to these rules, and one draw needn't show every extreme that they name: `migrate_to`: the 16 requests that leave one replica name 16 different target replicas, and one target replica is named by every replica. `prompt_pieces`: piece numbers never fall along a replica's prompt tokens; a piece has at most 320 tokens, and some piece exactly that many.
All inputs are finite; a program needn't handle non-finite values.
Results may differ from a plain program's by a relative error of at most 0.014.
Values may be sent and summed in bfloat16 or wider, within the bound.
No kernel may reach another device: no remote copies, remote signals or barrier semaphores. Data moves between devices by JAX's collectives and lax.ppermute only.
A program may use at most 128 MiB of HBM per device.

v0:
```python
import jax
import jax.numpy as jnp
from jax import lax
from jax.sharding import PartitionSpec as P

HEAD_DIM = 128
CAP = 1
EPSILON = 1e-05


def layer_norm(values, norm_gain, norm_bias):
    wide = values.astype(jnp.float32)
    center = jnp.mean(wide, axis=-1, keepdims=True)
    spread = jnp.mean(jnp.square(wide - center), axis=-1, keepdims=True)
    scaled = (wide - center) * lax.rsqrt(spread + EPSILON)
    return (scaled * norm_gain + norm_bias).astype(jnp.bfloat16)


def decode_partial(
    rows, cache, live, position, norm_gain, norm_bias, qkv_weight, qkv_bias, out_weight
):
    count = rows.shape[0]
    width = qkv_weight.shape[2]
    heads_here = width // HEAD_DIM
    length = cache.shape[2]
    normed = layer_norm(rows, norm_gain, norm_bias)
    projected = jnp.einsum("rd,cde->cre", normed, qkv_weight, preferred_element_type=jnp.float32)
    queries = (projected[0] + qkv_bias[0]).astype(jnp.bfloat16).reshape(count, heads_here, HEAD_DIM)
    key_new = (projected[1] + qkv_bias[1]).astype(jnp.bfloat16)
    value_new = (projected[2] + qkv_bias[2]).astype(jnp.bfloat16)
    old_keys = cache[:, 0].reshape(count, length, heads_here, HEAD_DIM)
    old_values = cache[:, 1].reshape(count, length, heads_here, HEAD_DIM)
    scale = HEAD_DIM ** (-0.5)
    scores = (
        jnp.einsum("rhe,rlhe->rhl", queries, old_keys, preferred_element_type=jnp.float32) * scale
    )
    own = (
        jnp.sum(
            queries.astype(jnp.float32)
            * key_new.astype(jnp.float32).reshape(count, heads_here, HEAD_DIM),
            axis=-1,
        )
        * scale
    )
    scores = jnp.where(live[:, None, :], scores, -1e30)
    highest = jnp.maximum(jnp.max(scores, axis=-1), own)
    weights = jnp.exp(scores - highest[..., None])
    own_weight = jnp.exp(own - highest)
    total = jnp.sum(weights, axis=-1) + own_weight
    probs = (weights / total[..., None]).astype(jnp.bfloat16)
    own_prob = (own_weight / total).astype(jnp.bfloat16)
    context = jnp.einsum("rhl,rlhe->rhe", probs, old_values, preferred_element_type=jnp.float32)
    context = context + own_prob.astype(jnp.float32)[..., None] * value_new.astype(
        jnp.float32
    ).reshape(count, heads_here, HEAD_DIM)
    context = context.reshape(count, width).astype(jnp.bfloat16)
    partial_value = jnp.dot(context, out_weight, preferred_element_type=jnp.float32)
    written = (jnp.arange(length)[None, :] == position[:, None])[:, :, None]
    new_keys = jnp.where(written, key_new[:, None, :], cache[:, 0])
    new_values = jnp.where(written, value_new[:, None, :], cache[:, 1])
    return (partial_value, jnp.stack([new_keys, new_values], axis=1))


def on_device(
    prompt_rows,
    prompt_pieces,
    decode_rows,
    request_ages,
    migrate_to,
    past_cache,
    norm_gain,
    norm_bias,
    qkv_weight,
    qkv_bias,
    out_weight,
    out_bias,
):
    rep_count = lax.axis_size("rep")
    width = qkv_weight.shape[2]
    heads_here = width // HEAD_DIM
    length = past_cache.shape[2]
    leaving = migrate_to.shape[0]
    staying = decode_rows.shape[0] - leaving
    slot_count = rep_count * CAP
    normed = layer_norm(lax.all_gather(prompt_rows, "tp", axis=0, tiled=True), norm_gain, norm_bias)
    projected = jnp.einsum("rd,cde->cre", normed, qkv_weight, preferred_element_type=jnp.float32)
    total_rows = projected.shape[1]
    queries = (projected[0] + qkv_bias[0]).astype(jnp.bfloat16)
    key_rows = (projected[1] + qkv_bias[1]).astype(jnp.bfloat16)
    value_rows = (projected[2] + qkv_bias[2]).astype(jnp.bfloat16)
    head_q = queries.reshape(total_rows, heads_here, HEAD_DIM)
    head_k = key_rows.reshape(total_rows, heads_here, HEAD_DIM)
    head_v = value_rows.reshape(total_rows, heads_here, HEAD_DIM)
    scores = jnp.einsum(
        "qhe,khe->hqk", head_q, head_k, preferred_element_type=jnp.float32
    ) * HEAD_DIM ** (-0.5)
    pieces = prompt_pieces[0]
    position = jnp.arange(total_rows)
    allowed = (pieces[:, None] == pieces[None, :]) & (position[None, :] <= position[:, None])
    scores = jnp.where(allowed[None], scores, -1e30)
    highest = jnp.max(scores, axis=-1, keepdims=True)
    weights = jnp.exp(scores - highest)
    probs = (weights / jnp.sum(weights, axis=-1, keepdims=True)).astype(jnp.bfloat16)
    context = jnp.einsum("hqk,khe->qhe", probs, head_v, preferred_element_type=jnp.float32)
    context = context.reshape(total_rows, width).astype(jnp.bfloat16)
    attended = lax.psum_scatter(
        jnp.dot(context, out_weight, preferred_element_type=jnp.float32).astype(jnp.bfloat16),
        "tp",
        scatter_dimension=0,
        tiled=True,
    ).astype(jnp.float32)
    prompt_out = (prompt_rows.astype(jnp.float32) + attended + out_bias).astype(jnp.bfloat16)
    prompt_cache = jnp.stack([key_rows, value_rows])
    targets = migrate_to[:, 0]
    onehot = (targets[:, None] == jnp.arange(rep_count)[None, :]).astype(jnp.float32)
    lower = (jnp.arange(leaving)[:, None] > jnp.arange(leaving)[None, :]).astype(jnp.float32)
    earlier = jnp.dot(lower, onehot)
    rank = jnp.sum(earlier * onehot, axis=1).astype(jnp.int32)
    slot = targets * CAP + rank
    placing = (jnp.arange(slot_count)[:, None] == slot[None, :]).astype(jnp.bfloat16)
    cells = jnp.arange(length)
    live = cells[None, :] < request_ages[:, None]
    partial_value, updated = decode_partial(
        decode_rows,
        past_cache,
        live,
        request_ages,
        norm_gain,
        norm_bias,
        qkv_weight,
        qkv_bias,
        out_weight,
    )
    summed = lax.psum(partial_value.astype(jnp.bfloat16), "tp").astype(jnp.float32)
    decode_out = (decode_rows.astype(jnp.float32) + summed + out_bias).astype(jnp.bfloat16)
    kept_out = decode_out[:staying]
    kept_cache = updated[:staying]
    send_cache = jnp.einsum(
        "so,oklh->sklh", placing, updated[staying:], preferred_element_type=jnp.float32
    ).astype(jnp.bfloat16)
    send_rows = jnp.dot(placing, decode_out[staying:], preferred_element_type=jnp.float32).astype(
        jnp.bfloat16
    )
    moved_cache, moved_out = (
        lax.all_to_all(send_cache, "rep", split_axis=0, concat_axis=0, tiled=True),
        lax.all_to_all(send_rows, "rep", split_axis=0, concat_axis=0, tiled=True),
    )
    return (prompt_out, prompt_cache, kept_out, kept_cache, moved_out, moved_cache)


def solution(mesh):
    placed = (
        P(("rep", "tp"), None),
        P("rep", None),
        P("rep", None),
        P("rep"),
        P("rep", None),
        P("rep", None, None, "tp"),
        P(),
        P(),
        P(None, None, "tp"),
        P(None, "tp"),
        P("tp", None),
        P(),
    )
    return jax.shard_map(
        on_device,
        mesh=mesh,
        in_specs=placed,
        out_specs=(
            P(("rep", "tp"), None),
            P(None, "rep", "tp"),
            P("rep", None),
            P("rep", None, None, "tp"),
            P("rep", None),
            P("rep", None, None, "tp"),
        ),
        check_vma=False,
    )
```

profile of v0, /device:TPU:8, one launch (start us, length us, event | category | flops | bytes accessed | tf_op | source)
XLA Modules:
  0.0 225.0 jit_solution(8399299144730349695)
XLA Ops:
  7.2 0.7 all-gather.2.cloned.1.call-update
  8.0 0.8 iota_compare_fusion.1
  8.9 1.0 convert_reduce_fusion.1
  10.0 1.1 fusion.32
  11.1 1.6 convolution_bitcast_fusion
  13.1 5.5 %fusion.71 = (bf16[40,1,128,256]{3,2,1,0:T(8,128)(2,1)}, bf16[40,1,128,256]{3,2,1,0:T(8,128)(2,1)}) fusion(bf16[40,2,128,256]{3,2,1,0:T(8,128)(2,1)} %param.17), kind=kLoop, calls=%fused_computation.117 | loop fusion | bytes 10485760 | tf_op jit(solution)/shard_map/slice | solution.py:31
  18.6 4.4 %copy.84 = bf16[40,1,128,256]{2,3,0,1:T(8,128)(2,1)} copy(bf16[40,1,128,256]{3,2,1,0:T(8,128)(2,1)} %get-tuple-element.36) | data formatting | bytes 5242880 | tf_op jit(solution)/shard_map/reshape;squeeze | solution.py:31
  23.0 2.6 %fusion.53 = f32[40,2,1,128]{3,2,1,0:T(1,128)S(1)} fusion(bf16[40,128,2,128]{1,3,2,0:T(8,128)(2,1)} %bitcast.75, bf16[40,2,128,1]{2,1,0,3:T(2,128)(2,1)S(1)} %get-tuple-element.49), kind=kOutput, calls=%fused_computation.82 | convolution fusion | flops 2621440 | bytes 2682880 | tf_op jit(solution)/shard_map/rhe,rlhe->rhl/dot_general | solution.py:35
  26.1 4.9 %reshape.266 = bf16[40,128,2,128]{3,2,1,0:T(2,128)(2,1)} reshape(bf16[40,1,128,256]{3,2,1,0:T(8,128)(2,1)} %get-tuple-element.37) | data formatting | bytes 5242880 | tf_op jit(solution)/shard_map/reshape;squeeze | solution.py:32
  31.1 4.4 %fusion.11 = f32[40,2,1,128]{3,2,1,0:T(1,128)S(1)} fusion(bf16[40,2,128,1]{2,0,1,3:T(8,128)(2,1)S(1)} %fusion.59, bf16[40,128,2,128]{3,2,1,0:T(2,128)(2,1)} %reshape.266), kind=kOutput, calls=%fused_computation.20 | convolution fusion | flops 2621440 | bytes 2682880 | tf_op jit(solution)/shard_map/rhl,rlhe->rhe/dot_general | solution.py:52
  35.7 1.0 convolution_convert_fusion.2
  36.6 0.2 reduce-scatter.2.cloned.1.call-start
  36.9 0.3 fusion.29
  37.2 1.0 fusion.23
  38.3 8.5 %broadcast_select_fusion = (bf16[40,1,128,256]{3,0,2,1:T(8,128)(2,1)}, bf16[40,1,128,256]{3,0,2,1:T(8,128)(2,1)}) fusion(pred[40,128]{0,1:T(8,128)(4,1)S(1)} %get-tuple-element.57, bf16[40,256]{1,0:T(8,128)(2,1)S(1)} %get-tuple-element.43, bf16[40,1,128,256]{3,2,1,0:T(8,128)(2,1)} %get-tuple-element.37, bf16[40,1,128,256]{3,2,1,0:T(8,128)(2,1)} %get-tuple-element.36, ...), kind=kLoop, calls=%fused_computation.26 | loop fusion | flops 2621440 | bytes 10531840 | tf_op jit(solution)/shard_map/jit(_where)/select_n | solution.py:60
  46.8 8.3 %all-gather.2.cloned.1.call-done = bf16[640,2048]{1,0:T(8,128)(2,1)} async-done(((bf16[80,2048]{1,0:T(8,128)(2,1)}), bf16[640,2048]{1,0:T(8,128)(2,1)}) %all-gather.2.cloned.1.call-update) | async-done | bytes 2621456 | tf_op jit(solution)/shard_map/all_gather | solution.py:85
  55.1 2.3 %convert_reduce_fusion = f32[640]{0:T(1024)S(1)} fusion(bf16[640,2048]{1,0:T(8,128)(2,1)} %all-gather.2.cloned.1.call-done), kind=kLoop, calls=%fused_computation.2 | loop fusion | flops 2620800 | bytes 2624000 | tf_op jit(solution)/shard_map/reduce_sum | solution.py:13
  57.4 0.2 copy-done.3
  57.6 0.8 fusion.3
  58.4 3.1 %fusion.25 = f32[3,640,256]{1,2,0:T(8,128)S(1)} fusion(bf16[3,2048,256]{2,1,0:T(8,128)(2,1)S(1)} %copy-done, bf16[640,2048]{1,0:T(8,128)(2,1)S(1)} %copy-done.3, f32[2048]{0:T(1024)S(1)} %copy-done.12, f32[2048]{0:T(1024)S(1)} %copy-done.13, f32[640]{0:T(1024)S(1)} %add_rsqrt_fusion, f32[640]{0:T(1024)S(1)} %broadcast_multiply_fusion), kind=kOutput, calls=%fused_computation.39 | convolution fusion | flops 2021130240 | bytes 7754752 | tf_op jit(solution)/shard_map/rd,cde->cre/dot_general | solution.py:86
  61.5 0.2 add_convert_fusion.1
  61.7 0.2 copy.64
  62.0 0.2 copy.63
  62.2 0.6 fusion.38
  62.8 0.4 copy-done.10
  63.2 2.0 fusion.74
  65.2 0.5 fusion.28
  65.7 0.7 copy-done.5
  66.4 2.4 %convolution_convert_fusion = bf16[640,2048]{1,0:T(8,128)(2,1)} fusion(bf16[640,256]{0,1:T(8,128)(2,1)S(1)} %bitcast.78, bf16[256,2048]{1,0:T(8,128)(2,1)S(1)} %copy-done.5), kind=kOutput, calls=%fused_computation.14 | convolution fusion | flops 672399360 | bytes 3997696 | tf_op jit(solution)/shard_map/dot_general | solution.py:107
  68.9 60.0 %all-reduce.2.cloned.1.call-done = bf16[40,2048]{1,0:T(8,128)(2,1)} async-done(((bf16[40,2048]{1,0:T(8,128)(2,1)}), bf16[40,2048]{1,0:T(8,128)(2,1)}) %all-reduce.2.cloned.1.call-update) | async-done | bytes 163856 | tf_op jit(solution)/shard_map/psum | solution.py:134
  128.8 1.0 fusion.37
  129.8 0.7 copy-done.8
  130.5 0.3 fusion.18
  130.8 0.5 broadcast.160
  131.3 1.3 reduce.1
  132.6 1.6 reshape.267
  134.3 7.4 %all-to-all-start = ((bf16[32,2,1024]{2,1,0:T(2,128)(2,1)}), bf16[32,2,1024]{2,1,0:T(2,128)(2,1)S(1)}, u32[]{:S(2)}, u32[]{:S(2)}) async-start(bf16[32,2,1024]{2,1,0:T(2,128)(2,1)} %reshape.267), calls=%async_computation.1 | async-start | bytes 262144 | tf_op jit(solution)/shard_map/all_to_all | solution.py:146
  141.7 2.6 %convolution_convert_fusion.1 = bf16[32,2,128,256]{3,0,2,1:T(8,128)(2,1)S(1)} fusion(bf16[40,1,128,256]{3,0,2,1:T(8,128)(2,1)S(1)} %copy-done.2, bf16[40,1,128,256]{3,0,2,1:T(8,128)(2,1)} %get-tuple-element.51, s32[16]{0:T(128)S(1)} %convert_add_fusion.1), kind=kOutput, calls=%fused_computation.16 | convolution fusion | flops 73400832 | bytes 9437248 | tf_op jit(solution)/shard_map/so,oklh->sklh/dot_general | solution.py:138
  144.3 4.4 %copy.72 = bf16[32,2,128,256]{3,2,1,0:T(8,128)(2,1)} copy(bf16[32,2,128,256]{3,0,2,1:T(8,128)(2,1)S(1)} %convolution_convert_fusion.1) | data formatting | bytes 8388608 | tf_op jit(solution)/shard_map/convert_element_type | solution.py:140
  148.7 7.4 %all-to-all-start.1 = ((bf16[32,2,128,256]{3,2,1,0:T(8,128)(2,1)}), bf16[32,2,128,256]{3,2,1,0:T(8,128)(2,1)}, u32[]{:S(2)}, u32[]{:S(2)}) async-start(bf16[32,2,128,256]{3,2,1,0:T(8,128)(2,1)} %copy.72), calls=%async_computation.2 | async-start | bytes 8388608 | tf_op jit(solution)/shard_map/all_to_all | solution.py:145
  156.2 1.6 fusion.7
  157.8 2.4 %copy.74 = bf16[24,2,128,256]{3,2,1,0:T(8,128)(2,1)} copy(bf16[24,2,128,256]{3,0,2,1:T(8,128)(2,1)S(1)} %fusion.7) | data formatting | bytes 6291456
  160.1 0.6 slice.71
  160.9 0.7 copy.116
  161.6 49.1 %all-to-all-done.1 = bf16[32,2,128,256]{3,2,1,0:T(8,128)(2,1)} async-done(((bf16[32,2,128,256]{3,2,1,0:T(8,128)(2,1)}), bf16[32,2,128,256]{3,2,1,0:T(8,128)(2,1)}, u32[]{:S(2)}, u32[]{:S(2)}) %all-to-all-start.1) | async-done | bytes 4194336 | tf_op jit(solution)/shard_map/all_to_all | solution.py:145
  210.8 1.1 copy.73
  211.9 1.8 add_convert_fusion.2
  213.7 4.8 %copy.120 = bf16[32,2,128,256]{3,2,1,0:T(8,128)(2,1)} copy(bf16[32,2,128,256]{3,2,1,0:T(8,128)(2,1)} %all-to-all-done.1) | data formatting | bytes 8388608
  (60 shorter events, 1.4 us)
Async XLA Ops:
  7.2 4.0 %copy-start = (bf16[3,2048,256]{2,1,0:T(8,128)(2,1)S(1)}, bf16[3,2048,256]{2,1,0:T(8,128)(2,1)}, u32[]{:S(2)}) copy-start(bf16[3,2048,256]{2,1,0:T(8,128)(2,1)} %param.20) | copy-start | bytes 9437188
  7.2 5.7 %copy-start.15 = (f32[3,256]{1,0:T(4,128)S(1)}, f32[3,256]{1,0:T(4,128)}, u32[]{:S(2)}) copy-start(f32[3,256]{1,0:T(4,128)} %param.21) | copy-start | bytes 9220
  7.2 47.9 %all-gather.2.cloned.1.call-start = ((), (), s32[]{:S(2)}) async-start(), calls=%async_computation.3 | async-start | bytes 2949120 | tf_op jit(solution)/shard_map/all_gather | solution.py:85
  7.9 120.9 %all-reduce.2.cloned.1.call-start = ((), (), s32[]{:S(2)}) async-start(), calls=%async_computation.5 | async-start | bytes 327680 | tf_op jit(solution)/shard_map/psum | solution.py:134
  31.1 4.6 %copy-start.4 = (bf16[256,2048]{1,0:T(8,128)(2,1)S(1)}, bf16[256,2048]{1,0:T(8,128)(2,1)}, u32[]{:S(2)}) copy-start(bf16[256,2048]{1,0:T(8,128)(2,1)} %param.22) | copy-start | bytes 3145732
  31.1 5.8 %copy-start.16 = (s32[16,1]{0,1:T(1,128)S(1)}, s32[16,1]{0,1:T(1,128)}, u32[]{:S(2)}) copy-start(s32[16,1]{0,1:T(1,128)} %param.16) | copy-start | bytes 196
  31.1 6.1 %copy-start.14 = (s32[1,640]{1,0:T(1,128)S(1)}, s32[1,640]{1,0:T(1,128)}, u32[]{:S(2)}) copy-start(s32[1,640]{1,0:T(1,128)} %param.13) | copy-start | bytes 7684
  36.6 175.2 %reduce-scatter.2.cloned.1.call-start = ((), (), s32[]{:S(2)}) async-start(), calls=%async_computation.4 | async-start | bytes 2949120 | tf_op jit(solution)/shard_map/reduce_scatter | solution.py:106
  46.8 11.7 %copy-start.12 = (f32[2048]{0:T(1024)S(1)}, f32[2048]{0:T(1024)}, u32[]{:S(2)}) copy-start(f32[2048]{0:T(1024)} %param.19) | copy-start | bytes 24580
  55.1 2.5 %copy-start.3 = (bf16[640,2048]{1,0:T(8,128)(2,1)S(1)}, bf16[640,2048]{1,0:T(8,128)(2,1)}, u32[]{:S(2)}) copy-start(bf16[640,2048]{1,0:T(8,128)(2,1)} %all-gather.2.cloned.1.call-done) | copy-start | bytes 7864324
  55.1 3.4 %copy-start.13 = (f32[2048]{0:T(1024)S(1)}, f32[2048]{0:T(1024)}, u32[]{:S(2)}) copy-start(f32[2048]{0:T(1024)} %param.18) | copy-start | bytes 24580
  62.2 1.0 copy-start.10
  65.2 1.2 copy-start.5
  66.4 62.4 %copy-start.6 = (bf16[40,2048]{1,0:T(8,128)(2,1)S(1)}, bf16[40,2048]{1,0:T(8,128)(2,1)}, u32[]{:S(2)}) copy-start(bf16[40,2048]{1,0:T(8,128)(2,1)} %param.14) | copy-start | bytes 491524
  66.4 62.4 %copy-start.11 = (f32[2048]{0:T(1024)S(1)}, f32[2048]{0:T(1024)}, u32[]{:S(2)}) copy-start(f32[2048]{0:T(1024)} %param.23) | copy-start | bytes 24580
  68.8 72.9 %copy-start.2 = (bf16[40,1,128,256]{3,0,2,1:T(8,128)(2,1)S(1)}, bf16[40,1,128,256]{3,0,2,1:T(8,128)(2,1)}, u32[]{:S(2)}) copy-start(bf16[40,1,128,256]{3,0,2,1:T(8,128)(2,1)} %get-tuple-element.50) | copy-start | bytes 7864324
  129.8 0.7 copy-start.8
  134.3 14.5 %all-to-all-start = ((bf16[32,2,1024]{2,1,0:T(2,128)(2,1)}), bf16[32,2,1024]{2,1,0:T(2,128)(2,1)S(1)}, u32[]{:S(2)}, u32[]{:S(2)}) async-start(bf16[32,2,1024]{2,1,0:T(2,128)(2,1)} %reshape.267), calls=%async_computation.1 | async-start | bytes 262144 | tf_op jit(solution)/shard_map/all_to_all | solution.py:146
  148.7 62.0 %all-to-all-start.1 = ((bf16[32,2,128,256]{3,2,1,0:T(8,128)(2,1)}), bf16[32,2,128,256]{3,2,1,0:T(8,128)(2,1)}, u32[]{:S(2)}, u32[]{:S(2)}) async-start(bf16[32,2,128,256]{3,2,1,0:T(8,128)(2,1)} %copy.72), calls=%async_computation.2 | async-start | bytes 8388608 | tf_op jit(solution)/shard_map/all_to_all | solution.py:145
  157.8 2.4 %copy-start.9 = (bf16[40,2048]{1,0:T(8,128)(2,1)S(1)}, bf16[40,2048]{1,0:T(8,128)(2,1)}, u32[]{:S(2)}) copy-start(bf16[40,2048]{1,0:T(8,128)(2,1)} %copy-done.8) | copy-start | bytes 491524
  160.1 51.7 %copy-start.7 = (bf16[80,2048]{1,0:T(8,128)(2,1)S(1)}, bf16[80,2048]{1,0:T(8,128)(2,1)}, u32[]{:S(2)}) copy-start(bf16[80,2048]{1,0:T(8,128)(2,1)} %param.12) | copy-start | bytes 983044
  213.7 4.9 %copy-start.1 = (bf16[3,2048,256]{2,1,0:T(8,128)(2,1)S(1)}, bf16[3,2048,256]{2,1,0:T(8,128)(2,1)}, u32[]{:S(2)}) copy-start(bf16[3,2048,256]{2,1,0:T(8,128)(2,1)} %param.20) | copy-start | bytes 9437188
Sparse Core Ops, SparseCore 0:
  9.8 45.1 all-gather.1
  58.0 70.8 all-reduce.1
  131.6 42.1 reduce-scatter.1
where the time goes:
time: 226 us; the launch traced here: 225 us
  waiting for transfers between devices  118 us (52%)
  local copies, waits for them, and re-layouts  34.1 us (15%)
  other arithmetic  24.3 us (11%)
  matrix products  19.4 us (9%)
  starting transfers between devices  15.1 us (7%)
  between operations  14.1 us (6%)
    psum x1, waiting for transfers between devices, on_device(): lax.psum(partial_value.astype(jnp.bfloat16), 'tp').astype(jnp.float32)  60 us
    all_to_all x1, waiting for transfers between devices, on_device(): lax.all_to_all(send_cache, 'rep', split_axis=0, concat_axis=0, tiled=True)  49.1 us
    unnamed x40, local copies, waits for them, and re-layouts  12.8 us
    select_n x1, other arithmetic, decode_partial(): new_values = jnp.where(written, value_new[:, None, :], cache[:, 1])  8.49 us
    all_gather x1, waiting for transfers between devices, on_device(): lax.all_gather(prompt_rows, 'tp', axis=0, tiled=True)  8.31 us
    all_to_all x1, starting transfers between devices, on_device(): lax.all_to_all(send_cache, 'rep', split_axis=0, concat_axis=0, tiled=True)  7.44 us
    all_to_all x1, starting transfers between devices, on_device(): lax.all_to_all(send_rows, 'rep', split_axis=0, concat_axis=0, tiled=True)  7.41 us
    slice x1, local copies, waits for them, and re-layouts, decode_partial(): old_keys = cache[:, 0].reshape(count, length, heads_here, HEAD_DIM)  5.54 us
  transfers between devices with their start and end apart: 5, of which 3 were waited for; matrix products, arithmetic and copies ran while one was open for 31% of the time, Pallas kernels for 0%

commit v1 on v0

--- a/solution.py
+++ b/solution.py
@@ -6,6 +6,27 @@
 HEAD_DIM = 128
 CAP = 1
 EPSILON = 1e-05
+
+
+def gather_around(x, axis, dim):
+    size, index, extent = (lax.axis_size(axis), lax.axis_index(axis), x.shape[dim])
+    right = [(i, (i + 1) % size) for i in range(size)]
+    behind = [(i, (i - 1) % size) for i in range(size)]
+    out = jnp.zeros((*x.shape[:dim], size * extent, *x.shape[dim + 1 :]), x.dtype)
+    out = lax.dynamic_update_slice_in_dim(out, x, index * extent, axis=dim)
+    from_left = from_right = x
+    half = size // 2
+    for step in range(1, half + 1):
+        from_left = lax.ppermute(from_left, axis, right)
+        out = lax.dynamic_update_slice_in_dim(
+            out, from_left, (index - step) % size * extent, axis=dim
+        )
+        if step < size - half:
+            from_right = lax.ppermute(from_right, axis, behind)
+            out = lax.dynamic_update_slice_in_dim(
+                out, from_right, (index + step) % size * extent, axis=dim
+            )
+    return out
 
 
 def layer_norm(values, norm_gain, norm_bias):
@@ -82,7 +103,7 @@
     leaving = migrate_to.shape[0]
     staying = decode_rows.shape[0] - leaving
     slot_count = rep_count * CAP
-    normed = layer_norm(lax.all_gather(prompt_rows, "tp", axis=0, tiled=True), norm_gain, norm_bias)
+    normed = layer_norm(gather_around(prompt_rows, "tp", 0), norm_gain, norm_bias)
     projected = jnp.einsum("rd,cde->cre", normed, qkv_weight, preferred_element_type=jnp.float32)
     total_rows = projected.shape[1]
     queries = (projected[0] + qkv_bias[0]).astype(jnp.bfloat16)

time: 226 us -> 211 us (0.934)
  waiting for transfers between devices: 118 us -> 76.7 us
  starting transfers between devices: 15.1 us -> 27.7 us
  local copies, waits for them, and re-layouts: 34.1 us -> 44.4 us
    psum x1, waiting for transfers between devices: 60 us -> 10.1 us  [on_device(): lax.psum(partial_value.astype(jnp.bfloat16), 'tp').astype(jnp.float32)]
    ppermute x0 -> x7, waiting for transfers between devices: none -> 18.6 us  [the longest x4 14.6 us: gather_around(): from_left = lax.ppermute(from_left, axis, right)]
    ppermute x0 -> x7, starting transfers between devices: none -> 12.8 us  [the longest x3 12.8 us: gather_around(): from_right = lax.ppermute(from_right, axis, behind)]
    all_gather x1 -> x0, waiting for transfers between devices: 8.31 us -> none  [on_device(): lax.all_gather(prompt_rows, 'tp', axis=0, tiled=True)]
    dynamic_update_slice x0 -> x8, local copies, waits for them, and re-layouts: none -> 7.95 us  [the longest x4 3.99 us: gather_around(): lax.dynamic_update_slice_in_dim(out, from_left, (index - step) % size * e...]
    unnamed x40 -> x38, local copies, waits for them, and re-layouts: 12.8 us -> 12.6 us
  transfers between devices with their start and end apart: 5 -> 11, of which waited for: 3 -> 5; matrix products, arithmetic and copies ran while one was open for 31% -> 39% of each run, Pallas kernels for 0% -> 0%
where the time goes in v1:
time: 211 us; the launch traced here: 210 us
  waiting for transfers between devices  76.7 us (36%)
  local copies, waits for them, and re-layouts  44.4 us (21%)
  starting transfers between devices  27.7 us (13%)
  other arithmetic  25.7 us (12%)
  matrix products  20.9 us (10%)
  between operations  14.4 us (7%)
    all_to_all x1, waiting for transfers between devices, on_device(): lax.all_to_all(send_cache, 'rep', split_axis=0, concat_axis=0, tiled=True)  47.9 us
    ppermute x4, waiting for transfers between devices, gather_around(): from_left = lax.ppermute(from_left, axis, right)  14.6 us
    ppermute x3, starting transfers between devices, gather_around(): from_right = lax.ppermute(from_right, axis, behind)  12.8 us
    unnamed x38, local copies, waits for them, and re-layouts  12.6 us
    psum x1, waiting for transfers between devices, on_device(): lax.psum(partial_value.astype(jnp.bfloat16), 'tp').astype(jnp.float32)  10.1 us
    select_n x1, other arithmetic, decode_partial(): new_values = jnp.where(written, value_new[:, None, :], cache[:, 1])  8.44 us
    all_to_all x1, starting transfers between devices, on_device(): lax.all_to_all(send_cache, 'rep', split_axis=0, concat_axis=0, tiled=True)  7.44 us
    all_to_all x1, starting transfers between devices, on_device(): lax.all_to_all(send_rows, 'rep', split_axis=0, concat_axis=0, tiled=True)  7.41 us
  transfers between devices with their start and end apart: 11, of which 5 were waited for; matrix products, arithmetic and copies ran while one was open for 39% of the time, Pallas kernels for 0%

profile of v1, /device:TPU:8, one launch (start us, length us, event | category | flops | bytes accessed | tf_op | source)
XLA Modules:
  0.0 209.7 jit_solution(7403555252862364519)
XLA Ops:
  7.2 5.9 %collective-permute-start.1 = (bf16[80,2048]{1,0:T(8,128)(2,1)}, bf16[80,2048]{1,0:T(8,128)(2,1)}, u32[]{:S(2)}, u32[]{:S(2)}) collective-permute-start(bf16[80,2048]{1,0:T(8,128)(2,1)} %param.12), channel_id=1, source_target_pairs={{0,7},{1,0},{2,1},{3,2},{4,3},{5,4},{6,5},{7,6},{8,15},{9,8},{10,9... | collective-permute-start | bytes 983048 | tf_op jit(solution)/shard_map/ppermute | solution.py:25
  13.2 1.0 convert_reduce_fusion.1
  14.2 1.1 fusion.32
  15.4 0.8 fusion.73
  17.0 1.6 convolution_bitcast_fusion
  18.9 5.5 %fusion.71 = (bf16[40,1,128,256]{3,2,1,0:T(8,128)(2,1)}, bf16[40,1,128,256]{3,2,1,0:T(8,128)(2,1)}) fusion(bf16[40,2,128,256]{3,2,1,0:T(8,128)(2,1)} %param.17), kind=kLoop, calls=%fused_computation.125 | loop fusion | bytes 10485760 | tf_op jit(solution)/shard_map/slice | solution.py:52
  24.4 4.4 %copy.84 = bf16[40,1,128,256]{2,3,0,1:T(8,128)(2,1)} copy(bf16[40,1,128,256]{3,2,1,0:T(8,128)(2,1)} %get-tuple-element.36) | data formatting | bytes 5242880 | tf_op jit(solution)/shard_map/reshape;squeeze | solution.py:52
  28.8 2.5 %fusion.53 = f32[40,2,1,128]{3,2,1,0:T(1,128)S(1)} fusion(bf16[40,128,2,128]{1,3,2,0:T(8,128)(2,1)} %bitcast.75, bf16[40,2,128,1]{2,1,0,3:T(2,128)(2,1)S(1)} %get-tuple-element.49), kind=kOutput, calls=%fused_computation.82 | convolution fusion | flops 2621440 | bytes 2682880 | tf_op jit(solution)/shard_map/rhe,rlhe->rhl/dot_general | solution.py:56
  31.8 4.9 %reshape.266 = bf16[40,128,2,128]{3,2,1,0:T(2,128)(2,1)} reshape(bf16[40,1,128,256]{3,2,1,0:T(8,128)(2,1)} %get-tuple-element.37) | data formatting | bytes 5242880 | tf_op jit(solution)/shard_map/reshape;squeeze | solution.py:53
  36.7 4.4 %fusion.11 = f32[40,2,1,128]{3,2,1,0:T(1,128)S(1)} fusion(bf16[40,2,128,1]{2,0,1,3:T(8,128)(2,1)S(1)} %fusion.59, bf16[40,128,2,128]{3,2,1,0:T(2,128)(2,1)} %reshape.266), kind=kOutput, calls=%fused_computation.20 | convolution fusion | flops 2621440 | bytes 2682880 | tf_op jit(solution)/shard_map/rhl,rlhe->rhe/dot_general | solution.py:73
  41.2 1.0 convolution_convert_fusion.2
  42.3 8.4 %broadcast_select_fusion = (bf16[40,1,128,256]{3,0,2,1:T(8,128)(2,1)}, bf16[40,1,128,256]{3,0,2,1:T(8,128)(2,1)}) fusion(pred[40,128]{0,1:T(8,128)(4,1)S(1)} %get-tuple-element.57, bf16[40,256]{1,0:T(8,128)(2,1)S(1)} %get-tuple-element.43, bf16[40,1,128,256]{3,2,1,0:T(8,128)(2,1)} %get-tuple-element.37, bf16[40,1,128,256]{3,2,1,0:T(8,128)(2,1)} %get-tuple-element.36, ...), kind=kLoop, calls=%fused_computation.26 | loop fusion | flops 2621440 | bytes 10531840 | tf_op jit(solution)/shard_map/jit(_where)/select_n | solution.py:81
  50.7 1.8 broadcast_in_dim.44
  52.6 0.7 constant_dynamic-update-slice_fusion.7
  53.4 1.0 fusion.23
  54.4 3.2 %collective-permute-start.3 = (bf16[80,2048]{1,0:T(8,128)(2,1)}, bf16[80,2048]{1,0:T(8,128)(2,1)S(1)}, u32[]{:S(2)}, u32[]{:S(2)}) collective-permute-start(bf16[80,2048]{1,0:T(8,128)(2,1)} %collective-permute-done.1), channel_id=1, source_target_pairs={{0,7},{1,0},{2,1},{3,2},{4,3},{5,4},{6,5},{7,6},{8,15},{9,8},{10,9... | collective-permute-start | bytes 983048 | tf_op jit(solution)/shard_map/ppermute | solution.py:25
  57.6 1.8 constant_dynamic-update-slice_fusion.6
  59.4 1.7 constant_dynamic-update-slice_fusion.5
  61.1 4.0 %collective-permute-done.3 = bf16[80,2048]{1,0:T(8,128)(2,1)S(1)} collective-permute-done((bf16[80,2048]{1,0:T(8,128)(2,1)}, bf16[80,2048]{1,0:T(8,128)(2,1)S(1)}, u32[]{:S(2)}, u32[]{:S(2)}) %collective-permute-start.3) | collective-permute-done | bytes 327712 | tf_op jit(solution)/shard_map/ppermute | solution.py:25
  65.2 3.6 %collective-permute-start.5 = (bf16[80,2048]{1,0:T(8,128)(2,1)S(1)}, bf16[80,2048]{1,0:T(8,128)(2,1)S(1)}, u32[]{:S(2)}, u32[]{:S(2)}) collective-permute-start(bf16[80,2048]{1,0:T(8,128)(2,1)S(1)} %collective-permute-done.3), channel_id=1, source_target_pairs={{0,7},{1,0},{2,1},{3,2},{4,3},{5,4},{6,5},{7,6},{8,15},{9,8},{10,9... | collective-permute-start | bytes 983048 | tf_op jit(solution)/shard_map/ppermute | solution.py:25
  68.7 0.7 constant_dynamic-update-slice_fusion.4
  69.5 0.7 constant_dynamic-update-slice_fusion.3
  70.2 7.8 %collective-permute-done.4 = bf16[80,2048]{1,0:T(8,128)(2,1)S(1)} collective-permute-done((bf16[80,2048]{1,0:T(8,128)(2,1)S(1)}, bf16[80,2048]{1,0:T(8,128)(2,1)S(1)}, u32[]{:S(2)}, u32[]{:S(2)}) %collective-permute-start.4) | collective-permute-done | bytes 327712 | tf_op jit(solution)/shard_map/ppermute | solution.py:20
  78.1 0.7 constant_dynamic-update-slice_fusion.2
  78.8 0.7 constant_dynamic-update-slice_fusion.1
  79.5 6.8 %collective-permute-done.6 = bf16[80,2048]{1,0:T(8,128)(2,1)S(1)} collective-permute-done((bf16[80,2048]{1,0:T(8,128)(2,1)S(1)}, bf16[80,2048]{1,0:T(8,128)(2,1)S(1)}, u32[]{:S(2)}, u32[]{:S(2)}) %collective-permute-start.6) | collective-permute-done | bytes 327712 | tf_op jit(solution)/shard_map/ppermute | solution.py:20
  86.3 0.7 constant_dynamic-update-slice_fusion
  87.1 2.2 %convert_reduce_fusion = f32[640]{0:T(1024)S(1)} fusion(bf16[640,2048]{1,0:T(8,128)(2,1)} %constant_dynamic-update-slice_fusion), kind=kLoop, calls=%fused_computation.2 | loop fusion | flops 2620800 | bytes 2624000 | tf_op jit(solution)/shard_map/reduce_sum | solution.py:34
  89.3 2.6 %fusion.3 = f32[640]{0:T(1024)S(1)} fusion(bf16[640,2048]{1,0:T(8,128)(2,1)} %constant_dynamic-update-slice_fusion, f32[640]{0:T(1024)S(1)} %broadcast_multiply_fusion), kind=kLoop, calls=%fused_computation.5 | loop fusion | flops 5242240 | bytes 2626560 | tf_op jit(solution)/shard_map/reduce_sum | solution.py:35
  91.9 4.7 %fusion.25 = f32[3,640,256]{1,2,0:T(8,128)S(1)} fusion(bf16[3,2048,256]{2,1,0:T(8,128)(2,1)S(1)} %copy-done, bf16[640,2048]{1,0:T(8,128)(2,1)} %constant_dynamic-update-slice_fusion, f32[2048]{0:T(1024)S(1)} %copy-done.12, f32[2048]{0:T(1024)S(1)} %copy-done.13, f32[640]{0:T(1024)S(1)} %add_rsqrt_fusion, f32[640]{0:T(1024)S(1)} %broadcast_multiply_fusion), kind=kOutput, calls=%fused_computation.39 | convolution fusion | flops 2021130240 | bytes 7754752 | tf_op jit(solution)/shard_map/rd,cde->cre/dot_general | solution.py:107
  98.3 2.0 fusion.74
  100.8 0.7 copy-done.4
  101.5 2.4 %convolution_convert_fusion = bf16[640,2048]{1,0:T(8,128)(2,1)} fusion(bf16[640,256]{0,1:T(8,128)(2,1)S(1)} %bitcast.78, bf16[256,2048]{1,0:T(8,128)(2,1)S(1)} %copy-done.4), kind=kOutput, calls=%fused_computation.14 | convolution fusion | flops 672399360 | bytes 3997696 | tf_op jit(solution)/shard_map/dot_general | solution.py:128
  104.2 10.1 %all-reduce.2.cloned.1.call-done = bf16[40,2048]{1,0:T(8,128)(2,1)} async-done(((bf16[40,2048]{1,0:T(8,128)(2,1)}), bf16[40,2048]{1,0:T(8,128)(2,1)}) %all-reduce.2.cloned.1.call-update) | async-done | bytes 163856 | tf_op jit(solution)/shard_map/psum | solution.py:155
  114.3 1.0 fusion.37
  116.8 1.3 reduce.1
  118.1 1.6 reshape.267
  119.8 7.4 %all-to-all-start = ((bf16[32,2,1024]{2,1,0:T(2,128)(2,1)}), bf16[32,2,1024]{2,1,0:T(2,128)(2,1)S(1)}, u32[]{:S(2)}, u32[]{:S(2)}) async-start(bf16[32,2,1024]{2,1,0:T(2,128)(2,1)} %reshape.267), calls=%async_computation.1 | async-start | bytes 262144 | tf_op jit(solution)/shard_map/all_to_all | solution.py:167
  127.2 2.6 %convolution_convert_fusion.1 = bf16[32,2,128,256]{3,0,2,1:T(8,128)(2,1)S(1)} fusion(bf16[40,1,128,256]{3,0,2,1:T(8,128)(2,1)S(1)} %copy-done.2, bf16[40,1,128,256]{3,0,2,1:T(8,128)(2,1)} %get-tuple-element.51, s32[16]{0:T(128)S(1)} %convert_add_fusion.1), kind=kOutput, calls=%fused_computation.16 | convolution fusion | flops 73400832 | bytes 9437248 | tf_op jit(solution)/shard_map/so,oklh->sklh/dot_general | solution.py:159
  129.8 4.4 %copy.72 = bf16[32,2,128,256]{3,2,1,0:T(8,128)(2,1)} copy(bf16[32,2,128,256]{3,0,2,1:T(8,128)(2,1)S(1)} %convolution_convert_fusion.1) | data formatting | bytes 8388608 | tf_op jit(solution)/shard_map/convert_element_type | solution.py:161
  134.2 7.4 %all-to-all-start.1 = ((bf16[32,2,128,256]{3,2,1,0:T(8,128)(2,1)}), bf16[32,2,128,256]{3,2,1,0:T(8,128)(2,1)}, u32[]{:S(2)}, u32[]{:S(2)}) async-start(bf16[32,2,128,256]{3,2,1,0:T(8,128)(2,1)} %copy.72), calls=%async_computation.2 | async-start | bytes 8388608 | tf_op jit(solution)/shard_map/all_to_all | solution.py:166
  141.7 1.6 fusion.7
  143.3 2.4 %copy.74 = bf16[24,2,128,256]{3,2,1,0:T(8,128)(2,1)} copy(bf16[24,2,128,256]{3,0,2,1:T(8,128)(2,1)S(1)} %fusion.7) | data formatting | bytes 6291456
  146.4 0.7 copy.116
  147.2 1.1 copy.73
  148.3 47.9 %all-to-all-done.1 = bf16[32,2,128,256]{3,2,1,0:T(8,128)(2,1)} async-done(((bf16[32,2,128,256]{3,2,1,0:T(8,128)(2,1)}), bf16[32,2,128,256]{3,2,1,0:T(8,128)(2,1)}, u32[]{:S(2)}, u32[]{:S(2)}) %all-to-all-start.1) | async-done | bytes 4194336 | tf_op jit(solution)/shard_map/all_to_all | solution.py:166
  196.2 1.8 add_convert_fusion.2
  198.0 4.8 %copy.128 = bf16[32,2,128,256]{3,2,1,0:T(8,128)(2,1)} copy(bf16[32,2,128,256]{3,2,1,0:T(8,128)(2,1)} %all-to-all-done.1) | data formatting | bytes 8388608
  (78 shorter events, 6.7 us)
Async XLA Ops:
  7.2 9.8 %copy-start = (bf16[3,2048,256]{2,1,0:T(8,128)(2,1)S(1)}, bf16[3,2048,256]{2,1,0:T(8,128)(2,1)}, u32[]{:S(2)}) copy-start(bf16[3,2048,256]{2,1,0:T(8,128)(2,1)} %param.20) | copy-start | bytes 9437188
  7.2 107.2 %all-reduce.2.cloned.1.call-start = ((), (), s32[]{:S(2)}) async-start(), calls=%async_computation.4 | async-start | bytes 327680 | tf_op jit(solution)/shard_map/psum | solution.py:155
  7.2 47.2 %collective-permute-start.1 = (bf16[80,2048]{1,0:T(8,128)(2,1)}, bf16[80,2048]{1,0:T(8,128)(2,1)}, u32[]{:S(2)}, u32[]{:S(2)}) collective-permute-start(bf16[80,2048]{1,0:T(8,128)(2,1)} %param.12), channel_id=1, source_target_pairs={{0,7},{1,0},{2,1},{3,2},{4,3},{5,4},{6,5},{7,6},{8,15},{9,8},{10,9... | collective-permute-start | bytes 983048 | tf_op jit(solution)/shard_map/ppermute | solution.py:25
  13.2 44.5 %collective-permute-start = (bf16[80,2048]{1,0:T(8,128)(2,1)}, bf16[80,2048]{1,0:T(8,128)(2,1)}, u32[]{:S(2)}, u32[]{:S(2)}) collective-permute-start(bf16[80,2048]{1,0:T(8,128)(2,1)} %param.12), channel_id=1, source_target_pairs={{0,1},{1,2},{2,3},{3,4},{4,5},{5,6},{6,7},{7,0},{8,9},{9,10},{10,1... | collective-permute-start | bytes 983048 | tf_op jit(solution)/shard_map/ppermute | solution.py:20
  36.7 4.5 %copy-start.3 = (bf16[256,2048]{1,0:T(8,128)(2,1)S(1)}, bf16[256,2048]{1,0:T(8,128)(2,1)}, u32[]{:S(2)}) copy-start(bf16[256,2048]{1,0:T(8,128)(2,1)} %param.22) | copy-start | bytes 3145732
  42.2 154.0 %reduce-scatter.2.cloned.1.call-start = ((), (), s32[]{:S(2)}) async-start(), calls=%async_computation.3 | async-start | bytes 2949120 | tf_op jit(solution)/shard_map/reduce_scatter | solution.py:127
  50.7 1.8 copy-start.6
  50.7 2.6 %copy-start.14 = (s32[1,640]{1,0:T(1,128)S(1)}, s32[1,640]{1,0:T(1,128)}, u32[]{:S(2)}) copy-start(s32[1,640]{1,0:T(1,128)} %param.13) | copy-start | bytes 7684
  54.4 10.7 %collective-permute-start.3 = (bf16[80,2048]{1,0:T(8,128)(2,1)}, bf16[80,2048]{1,0:T(8,128)(2,1)S(1)}, u32[]{:S(2)}, u32[]{:S(2)}) collective-permute-start(bf16[80,2048]{1,0:T(8,128)(2,1)} %collective-permute-done.1), channel_id=1, source_target_pairs={{0,7},{1,0},{2,1},{3,2},{4,3},{5,4},{6,5},{7,6},{8,15},{9,8},{10,9... | collective-permute-start | bytes 983048 | tf_op jit(solution)/shard_map/ppermute | solution.py:25
  57.6 11.1 %collective-permute-start.2 = (bf16[80,2048]{1,0:T(8,128)(2,1)}, bf16[80,2048]{1,0:T(8,128)(2,1)S(1)}, u32[]{:S(2)}, u32[]{:S(2)}) collective-permute-start(bf16[80,2048]{1,0:T(8,128)(2,1)} %collective-permute-done), channel_id=1, source_target_pairs={{0,1},{1,2},{2,3},{3,4},{4,5},{5,6},{6,7},{7,0},{8,9},{9,10},{10,1... | collective-permute-start | bytes 983048 | tf_op jit(solution)/shard_map/ppermute | solution.py:20
  65.2 13.6 %collective-permute-start.5 = (bf16[80,2048]{1,0:T(8,128)(2,1)S(1)}, bf16[80,2048]{1,0:T(8,128)(2,1)S(1)}, u32[]{:S(2)}, u32[]{:S(2)}) collective-permute-start(bf16[80,2048]{1,0:T(8,128)(2,1)S(1)} %collective-permute-done.3), channel_id=1, source_target_pairs={{0,7},{1,0},{2,1},{3,2},{4,3},{5,4},{6,5},{7,6},{8,15},{9,8},{10,9... | collective-permute-start | bytes 983048 | tf_op jit(solution)/shard_map/ppermute | solution.py:25
  68.7 9.3 %collective-permute-start.4 = (bf16[80,2048]{1,0:T(8,128)(2,1)S(1)}, bf16[80,2048]{1,0:T(8,128)(2,1)S(1)}, u32[]{:S(2)}, u32[]{:S(2)}) collective-permute-start(bf16[80,2048]{1,0:T(8,128)(2,1)S(1)} %collective-permute-done.2), channel_id=1, source_target_pairs={{0,1},{1,2},{2,3},{3,4},{4,5},{5,6},{6,7},{7,0},{8,9},{9,10},{10,1... | collective-permute-start | bytes 983048 | tf_op jit(solution)/shard_map/ppermute | solution.py:20
  78.0 8.3 %collective-permute-start.6 = (bf16[80,2048]{1,0:T(8,128)(2,1)S(1)}, bf16[80,2048]{1,0:T(8,128)(2,1)S(1)}, u32[]{:S(2)}, u32[]{:S(2)}) collective-permute-start(bf16[80,2048]{1,0:T(8,128)(2,1)S(1)} %collective-permute-done.4), channel_id=1, source_target_pairs={{0,1},{1,2},{2,3},{3,4},{4,5},{5,6},{6,7},{7,0},{8,9},{9,10},{10,1... | collective-permute-start | bytes 983048 | tf_op jit(solution)/shard_map/ppermute | solution.py:20
  87.1 4.8 %copy-start.12 = (f32[2048]{0:T(1024)S(1)}, f32[2048]{0:T(1024)}, u32[]{:S(2)}) copy-start(f32[2048]{0:T(1024)} %param.19) | copy-start | bytes 24580
  87.1 4.8 %copy-start.13 = (f32[2048]{0:T(1024)S(1)}, f32[2048]{0:T(1024)}, u32[]{:S(2)}) copy-start(f32[2048]{0:T(1024)} %param.18) | copy-start | bytes 24580
  97.3 1.0 copy-start.10
  100.3 1.2 copy-start.4
  101.5 2.4 %copy-start.15 = (s32[16,1]{0,1:T(1,128)S(1)}, s32[16,1]{0,1:T(1,128)}, u32[]{:S(2)}) copy-start(s32[16,1]{0,1:T(1,128)} %param.16) | copy-start | bytes 196
  101.5 12.9 %copy-start.5 = (bf16[40,2048]{1,0:T(8,128)(2,1)S(1)}, bf16[40,2048]{1,0:T(8,128)(2,1)}, u32[]{:S(2)}) copy-start(bf16[40,2048]{1,0:T(8,128)(2,1)} %param.14) | copy-start | bytes 491524
  103.9 10.4 %copy-start.11 = (f32[2048]{0:T(1024)S(1)}, f32[2048]{0:T(1024)}, u32[]{:S(2)}) copy-start(f32[2048]{0:T(1024)} %param.23) | copy-start | bytes 24580
  103.9 23.3 %copy-start.2 = (bf16[40,1,128,256]{3,0,2,1:T(8,128)(2,1)S(1)}, bf16[40,1,128,256]{3,0,2,1:T(8,128)(2,1)}, u32[]{:S(2)}) copy-start(bf16[40,1,128,256]{3,0,2,1:T(8,128)(2,1)} %get-tuple-element.50) | copy-start | bytes 7864324
  115.3 0.7 copy-start.8
  119.8 14.5 %all-to-all-start = ((bf16[32,2,1024]{2,1,0:T(2,128)(2,1)}), bf16[32,2,1024]{2,1,0:T(2,128)(2,1)S(1)}, u32[]{:S(2)}, u32[]{:S(2)}) async-start(bf16[32,2,1024]{2,1,0:T(2,128)(2,1)} %reshape.267), calls=%async_computation.1 | async-start | bytes 262144 | tf_op jit(solution)/shard_map/all_to_all | solution.py:167
  134.2 62.0 %all-to-all-start.1 = ((bf16[32,2,128,256]{3,2,1,0:T(8,128)(2,1)}), bf16[32,2,128,256]{3,2,1,0:T(8,128)(2,1)}, u32[]{:S(2)}, u32[]{:S(2)}) async-start(bf16[32,2,128,256]{3,2,1,0:T(8,128)(2,1)} %copy.72), calls=%async_computation.2 | async-start | bytes 8388608 | tf_op jit(solution)/shard_map/all_to_all | solution.py:166
  143.3 2.4 %copy-start.9 = (bf16[40,2048]{1,0:T(8,128)(2,1)S(1)}, bf16[40,2048]{1,0:T(8,128)(2,1)}, u32[]{:S(2)}) copy-start(bf16[40,2048]{1,0:T(8,128)(2,1)} %copy-done.8) | copy-start | bytes 491524
  145.6 50.6 %copy-start.7 = (bf16[80,2048]{1,0:T(8,128)(2,1)S(1)}, bf16[80,2048]{1,0:T(8,128)(2,1)}, u32[]{:S(2)}) copy-start(bf16[80,2048]{1,0:T(8,128)(2,1)} %param.12) | copy-start | bytes 983044
  198.0 4.9 %copy-start.1 = (bf16[3,2048,256]{2,1,0:T(8,128)(2,1)S(1)}, bf16[3,2048,256]{2,1,0:T(8,128)(2,1)}, u32[]{:S(2)}) copy-start(bf16[3,2048,256]{2,1,0:T(8,128)(2,1)} %param.20) | copy-start | bytes 9437188
Sparse Core Ops, SparseCore 0:
  42.4 71.9 all-reduce.1
  117.1 42.1 reduce-scatter.1
